TPU v7x, 256 devices: a whole 4x4x8 slice. The times are simulated.
256 devices in a mesh: dp: 32 (over x, y, core), shard: 8 (over z).
Axes of the slice: x: 4, y: 4, z: 8, core: 2. Of those that a mesh axis runs over, the one named last changes fastest.
Arguments:
- audio: bfloat16 [65536, 512], P(('dp', 'shard')), may hold values from -6 to 6
- cotangent: bfloat16 [65536, 512], P(('dp', 'shard')), may hold values from -6 to 6
- clip_lengths: int32 [256, 8], P(('dp', 'shard')), may hold values from 1 to 128, 256 in all within a row
- conv_weight: bfloat16 [3584, 512], P('shard'), may hold values from -0.09375 to 0.09375
- mix_weight: bfloat16 [512, 512], P('shard'), may hold values from -0.25 to 0.25
- conv_bias: float32 [512], replicated, may hold values from -3 to 3
- alpha_in: float32 [512], replicated, may hold values from 0.5 to 3
- alpha_mid: float32 [512], replicated, may hold values from 0.5 to 3
Outputs:
- in_grad: bfloat16 [65536, 512], P(('dp', 'shard'))
- conv_grad: float32 [3584, 512], P(('dp', 'shard'))
- mix_grad: float32 [512, 512], P(('dp', 'shard'))
- vector_grad: float32 [4, 512], P(None, ('dp', 'shard'))
Inputs may be any that keep to these rules, and one draw needn't show every extreme that they name: `clip_lengths`: each device's clip lengths sum to 256; the largest on each device is 128.
All inputs are finite; a program needn't handle non-finite values.
Results may differ from a plain program's by a relative error of at most 0.01.
Values may be sent and summed in bfloat16 or wider, within the bound.
No kernel may reach another device: no remote copies, remote signals or barrier semaphores. Data moves between devices by JAX's collectives and lax.ppermute only.
A program may use at most 64 MiB of HBM per device.

v0:
```python
import jax
import jax.numpy as jnp
from jax import lax
from jax.sharding import PartitionSpec as P

C = 512
TAPS = 7
DILATION_SIZE = 9


def shift_rows(block, tap_offset, fill):
    rows = block.shape[0]
    shift_amount = min(abs(tap_offset), rows)
    if shift_amount == 0:
        return block
    edge_padding = jnp.full((shift_amount,) + block.shape[1:], fill, block.dtype)
    if tap_offset > 0:
        return jnp.concatenate([block[shift_amount:], edge_padding], axis=0)
    return jnp.concatenate([edge_padding, block[: rows - shift_amount]], axis=0)


def clip_masks(lengths_row, rows):
    clip_ends = jnp.cumsum(lengths_row)
    position = jnp.arange(rows, dtype=jnp.int32)
    clip_id = jnp.sum((position[:, None] >= clip_ends[None, :]).astype(jnp.int32), axis=1)
    result = []
    for kernel_tap_index in range(TAPS):
        tap_offset = (kernel_tap_index - 3) * DILATION_SIZE
        result.append(shift_rows(clip_id, tap_offset, -1) == clip_id)
    return result


def snake_parts(value, alpha):
    sine = jnp.sin(alpha * value)
    double = jnp.sin(2.0 * alpha * value)
    return (
        value + sine * sine / alpha,
        1.0 + double,
        value * double / alpha - sine * sine / (alpha * alpha),
    )


def per_device(
    audio, cotangent, clip_lengths, conv_weight, mix_weight, conv_bias, alpha_in, alpha_mid
):
    rows = audio.shape[0]
    same_clip_flags = clip_masks(clip_lengths[0], rows)
    mix_full = lax.all_gather(mix_weight, "shard", axis=0, tiled=True)
    audio_f = audio.astype(jnp.float32)
    act_in, slope_in, dalpha_in = snake_parts(audio_f, alpha_in)
    first = act_in.astype(jnp.bfloat16)
    columns = []
    for kernel_tap_index in range(TAPS):
        tap_offset = (kernel_tap_index - 3) * DILATION_SIZE
        moved = shift_rows(first, tap_offset, 0)
        columns.append(
            jnp.where(same_clip_flags[kernel_tap_index][:, None], moved, jnp.zeros_like(moved))
        )
    unfolded = jnp.concatenate(columns, axis=1)
    product = jnp.dot(
        unfolded,
        lax.all_gather(conv_weight, "shard", axis=0, tiled=True),
        preferred_element_type=jnp.float32,
    )
    pre = product + conv_bias
    act_mid, slope_mid, dalpha_mid = snake_parts(pre, alpha_mid)
    second = act_mid.astype(jnp.bfloat16)
    mix_term = lax.dot_general(
        second, cotangent, (((0,), (0,)), ((), ())), preferred_element_type=jnp.float32
    )
    second_gradient = lax.dot_general(
        cotangent, mix_full, (((1,), (1,)), ((), ())), preferred_element_type=jnp.float32
    )
    d_pre = (second_gradient * slope_mid).astype(jnp.bfloat16)
    convolution_part = lax.dot_general(
        unfolded, d_pre, (((0,), (0,)), ((), ())), preferred_element_type=jnp.float32
    )
    d_unf = lax.dot_general(
        d_pre,
        lax.all_gather(conv_weight, "shard", axis=0, tiled=True),
        (((1,), (1,)), ((), ())),
        preferred_element_type=jnp.float32,
    ).astype(jnp.bfloat16)
    d_first = jnp.zeros((rows, C), jnp.float32)
    for kernel_tap_index in range(TAPS):
        tap_offset = (kernel_tap_index - 3) * DILATION_SIZE
        piece = d_unf[:, kernel_tap_index * C : (kernel_tap_index + 1) * C].astype(jnp.float32)
        piece = jnp.where(same_clip_flags[kernel_tap_index][:, None], piece, jnp.zeros_like(piece))
        d_first = d_first + shift_rows(piece, -tap_offset, 0.0)
    in_grad = (cotangent.astype(jnp.float32) + d_first * slope_in).astype(jnp.bfloat16)
    vectors = jnp.stack(
        [
            jnp.sum(d_pre.astype(jnp.float32), axis=0),
            jnp.sum(cotangent.astype(jnp.float32), axis=0),
            jnp.sum(d_first * dalpha_in, axis=0),
            jnp.sum(second_gradient * dalpha_mid, axis=0),
        ]
    )
    conv_grad, mix_grad, vector_grad = (
        lax.psum_scatter(convolution_part, ("dp", "shard"), scatter_dimension=0, tiled=True),
        lax.psum_scatter(mix_term, ("dp", "shard"), scatter_dimension=0, tiled=True),
        lax.psum_scatter(vectors, ("dp", "shard"), scatter_dimension=1, tiled=True),
    )
    return (in_grad, conv_grad, mix_grad, vector_grad)


def solution(mesh):
    placed = (
        P(("dp", "shard"), None),
        P(("dp", "shard"), None),
        P(("dp", "shard"), None),
        P("shard", None),
        P("shard", None),
        P(),
        P(),
        P(),
    )
    return jax.shard_map(
        per_device,
        mesh=mesh,
        in_specs=placed,
        out_specs=(
            P(("dp", "shard"), None),
            P(("dp", "shard"), None),
            P(("dp", "shard"), None),
            P(None, ("dp", "shard")),
        ),
        check_vma=False,
    )
```

profile of v0, /device:TPU:2, one launch (start us, length us, event | category | flops | bytes accessed | tf_op | source)
XLA Modules:
  0.0 1037.1 jit_solution(11425878607155914596)
XLA Ops:
  10.8 30.8 %all_gather.7 = bf16[512,512]{1,0:T(8,128)(2,1)S(1)} all-gather(bf16[64,512]{1,0:T(8,128)(2,1)} %param.12), channel_id=1, replica_groups=mesh['dp'=32,'shard'=8] {'shard'}, dimensions={0}, use_global_device_ids=true | all-gather | bytes 589824 | tf_op jit(solution)/shard_map/all_gather | solution.py:48
  41.6 2.8 fusion.8
  47.6 17.5 %all-gather.2.cloned.1.call-done = bf16[3584,512]{1,0:T(8,128)(2,1)} async-done(((bf16[448,512]{1,0:T(8,128)(2,1)}), bf16[3584,512]{1,0:T(8,128)(2,1)}) %all-gather.2.cloned.1.call-update) | async-done | bytes 3670032 | tf_op jit(solution)/shard_map/all_gather | solution.py:62
  65.0 3.1 convolution_add_fusion
  69.0 3.0 fusion.14
  72.0 4.9 convert_reduce_fusion.1
  77.0 4.1 fusion.23
  81.0 597.1 %fusion = f32[16,512]{1,0:T(8,128)S(1)} fusion(f32[3584,512]{1,0:T(8,128)} %fusion.23), kind=kCustom, calls=%all-reduce-scatter | all-reduce-scatter fusion | flops 2097153 | bytes 7372800
  685.9 3.2 convolution_convert_fusion
  689.2 4.0 collective-permute-start.31
  693.7 4.0 collective-permute-done.31
  697.7 51.7 %collective-permute-start.26 = (f32[16,512]{1,0:T(8,128)S(1)}, f32[16,512]{1,0:T(8,128)S(1)}, u32[]{:S(2)}, u32[]{:S(2)}) collective-permute-start(f32[16,512]{1,0:T(8,128)S(1)} %fusion), channel_id=1, source_target_pairs={{0,27},{1,28},{2,29},{3,30},{4,31},{5,32},{6,33},{7,34},{8,35},{9,... | collective-permute-start | bytes 98312
  753.4 43.3 %collective-permute-start.23 = (f32[16,512]{1,0:T(8,128)S(1)}, f32[16,512]{1,0:T(8,128)S(1)}, u32[]{:S(2)}, u32[]{:S(2)}) collective-permute-start(f32[16,512]{1,0:T(8,128)S(1)} %fusion), channel_id=1, source_target_pairs={{0,24},{1,25},{2,26},{3,27},{4,28},{5,29},{6,30},{7,31},{8,32},{9,... | collective-permute-start | bytes 98312
  796.7 3.6 collective-permute-start.22
  802.3 2.7 collective-permute-start.20
  805.1 5.1 collective-permute-start.19
  810.2 3.7 collective-permute-start.18
  817.8 2.9 collective-permute-start.15
  820.7 3.9 fusion.13
  824.6 3.1 collective-permute-start.14
  829.7 4.2 collective-permute-start.12
  833.9 5.1 collective-permute-start.11
  843.7 3.4 collective-permute-start.9
  851.1 4.4 collective-permute-start.6
  857.5 80.1 %all-reduce.20 = f32[4,512]{1,0:T(4,128)S(1)} all-reduce(f32[4,512]{1,0:T(4,128)S(1)} %pad_maximum_fusion), channel_id=4, replica_groups=mesh['dp'=32,'shard'=8] {'dp','shard'}, use_global_device_ids=true, to_apply=%region_8.9.clone | all-reduce | flops 2048 | bytes 16384
  937.6 4.4 collective-permute-start.4
  942.1 4.5 collective-permute-start.3
  949.0 3.3 collective-permute-start.1
  952.3 4.2 collective-permute-start
  959.4 3.0 collective-permute-done
  962.4 3.8 concatenate.76
  966.9 62.1 %all-reduce.24.cloned.1.call-done = f32[512,512]{1,0:T(8,128)} async-done(((f32[512,512]{1,0:T(8,128)}), f32[512,512]{1,0:T(8,128)}) %all-reduce.24.cloned.1.call-update) | async-done | bytes 1048592
  (95 shorter events, 45.5 us)
Async XLA Ops:
  7.2 57.9 %all-gather.2.cloned.1.call-start = ((), (), s32[]{:S(2)}) async-start(), calls=%async_computation | async-start | bytes 4128768 | tf_op jit(solution)/shard_map/all_gather | solution.py:62
  7.9 1021.1 %all-reduce.24.cloned.1.call-start = ((), (), s32[]{:S(2)}) async-start(), calls=%async_computation.1 | async-start | bytes 2097152
  678.2 71.2 %collective-permute-start.30 = (f32[16,512]{1,0:T(8,128)S(1)}, f32[16,512]{1,0:T(8,128)S(1)}, u32[]{:S(2)}, u32[]{:S(2)}) collective-permute-start(f32[16,512]{1,0:T(8,128)S(1)} %fusion), channel_id=1, source_target_pairs={{0,31},{1,32},{2,33},{3,34},{4,35},{5,36},{6,37},{7,38},{8,39},{9,... | collective-permute-start | bytes 98312
  680.1 71.3 %collective-permute-start.29 = (f32[16,512]{1,0:T(8,128)S(1)}, f32[16,512]{1,0:T(8,128)S(1)}, u32[]{:S(2)}, u32[]{:S(2)}) collective-permute-start(f32[16,512]{1,0:T(8,128)S(1)} %fusion), channel_id=1, source_target_pairs={{0,30},{1,31},{2,32},{3,33},{4,34},{5,35},{6,36},{7,37},{8,38},{9,... | collective-permute-start | bytes 98312
  682.0 71.4 %collective-permute-start.28 = (f32[16,512]{1,0:T(8,128)S(1)}, f32[16,512]{1,0:T(8,128)S(1)}, u32[]{:S(2)}, u32[]{:S(2)}) collective-permute-start(f32[16,512]{1,0:T(8,128)S(1)} %fusion), channel_id=1, source_target_pairs={{0,29},{1,30},{2,31},{3,32},{4,33},{5,34},{6,35},{7,36},{8,37},{9,... | collective-permute-start | bytes 98312
  684.0 112.7 %collective-permute-start.27 = (f32[16,512]{1,0:T(8,128)S(1)}, f32[16,512]{1,0:T(8,128)S(1)}, u32[]{:S(2)}, u32[]{:S(2)}) collective-permute-start(f32[16,512]{1,0:T(8,128)S(1)} %fusion), channel_id=1, source_target_pairs={{0,28},{1,29},{2,30},{3,31},{4,32},{5,33},{6,34},{7,35},{8,36},{9,... | collective-permute-start | bytes 98312
  697.7 102.6 %collective-permute-start.26 = (f32[16,512]{1,0:T(8,128)S(1)}, f32[16,512]{1,0:T(8,128)S(1)}, u32[]{:S(2)}, u32[]{:S(2)}) collective-permute-start(f32[16,512]{1,0:T(8,128)S(1)} %fusion), channel_id=1, source_target_pairs={{0,27},{1,28},{2,29},{3,30},{4,31},{5,32},{6,33},{7,34},{8,35},{9,... | collective-permute-start | bytes 98312
  749.4 52.9 %collective-permute-start.25 = (f32[16,512]{1,0:T(8,128)S(1)}, f32[16,512]{1,0:T(8,128)S(1)}, u32[]{:S(2)}, u32[]{:S(2)}) collective-permute-start(f32[16,512]{1,0:T(8,128)S(1)} %fusion), channel_id=1, source_target_pairs={{0,26},{1,27},{2,28},{3,29},{4,30},{5,31},{6,32},{7,33},{8,34},{9,... | collective-permute-start | bytes 98312
  751.5 53.6 %collective-permute-start.24 = (f32[16,512]{1,0:T(8,128)S(1)}, f32[16,512]{1,0:T(8,128)S(1)}, u32[]{:S(2)}, u32[]{:S(2)}) collective-permute-start(f32[16,512]{1,0:T(8,128)S(1)} %fusion), channel_id=1, source_target_pairs={{0,25},{1,26},{2,27},{3,28},{4,29},{5,30},{6,31},{7,32},{8,33},{9,... | collective-permute-start | bytes 98312
  753.4 56.8 %collective-permute-start.23 = (f32[16,512]{1,0:T(8,128)S(1)}, f32[16,512]{1,0:T(8,128)S(1)}, u32[]{:S(2)}, u32[]{:S(2)}) collective-permute-start(f32[16,512]{1,0:T(8,128)S(1)} %fusion), channel_id=1, source_target_pairs={{0,24},{1,25},{2,26},{3,27},{4,28},{5,29},{6,30},{7,31},{8,32},{9,... | collective-permute-start | bytes 98312
  796.7 17.2 %collective-permute-start.22 = (f32[16,512]{1,0:T(8,128)S(1)}, f32[16,512]{1,0:T(8,128)S(1)}, u32[]{:S(2)}, u32[]{:S(2)}) collective-permute-start(f32[16,512]{1,0:T(8,128)S(1)} %fusion), channel_id=1, source_target_pairs={{0,23},{1,24},{2,25},{3,26},{4,27},{5,28},{6,29},{7,30},{8,31},{9,... | collective-permute-start | bytes 98312
  800.3 15.6 %collective-permute-start.21 = (f32[16,512]{1,0:T(8,128)S(1)}, f32[16,512]{1,0:T(8,128)S(1)}, u32[]{:S(2)}, u32[]{:S(2)}) collective-permute-start(f32[16,512]{1,0:T(8,128)S(1)} %fusion), channel_id=1, source_target_pairs={{0,22},{1,23},{2,24},{3,25},{4,26},{5,27},{6,28},{7,29},{8,30},{9,... | collective-permute-start | bytes 98312
  802.3 15.6 %collective-permute-start.20 = (f32[16,512]{1,0:T(8,128)S(1)}, f32[16,512]{1,0:T(8,128)S(1)}, u32[]{:S(2)}, u32[]{:S(2)}) collective-permute-start(f32[16,512]{1,0:T(8,128)S(1)} %fusion), channel_id=1, source_target_pairs={{0,21},{1,22},{2,23},{3,24},{4,25},{5,26},{6,27},{7,28},{8,29},{9,... | collective-permute-start | bytes 98312
  805.1 19.5 %collective-permute-start.19 = (f32[16,512]{1,0:T(8,128)S(1)}, f32[16,512]{1,0:T(8,128)S(1)}, u32[]{:S(2)}, u32[]{:S(2)}) collective-permute-start(f32[16,512]{1,0:T(8,128)S(1)} %fusion), channel_id=1, source_target_pairs={{0,20},{1,21},{2,22},{3,23},{4,24},{5,25},{6,26},{7,27},{8,28},{9,... | collective-permute-start | bytes 98312
  810.2 17.4 %collective-permute-start.18 = (f32[16,512]{1,0:T(8,128)S(1)}, f32[16,512]{1,0:T(8,128)S(1)}, u32[]{:S(2)}, u32[]{:S(2)}) collective-permute-start(f32[16,512]{1,0:T(8,128)S(1)} %fusion), channel_id=1, source_target_pairs={{0,19},{1,20},{2,21},{3,22},{4,23},{5,24},{6,25},{7,26},{8,27},{9,... | collective-permute-start | bytes 98312
  814.0 15.7 %collective-permute-start.17 = (f32[16,512]{1,0:T(8,128)S(1)}, f32[16,512]{1,0:T(8,128)S(1)}, u32[]{:S(2)}, u32[]{:S(2)}) collective-permute-start(f32[16,512]{1,0:T(8,128)S(1)} %fusion), channel_id=1, source_target_pairs={{0,18},{1,19},{2,20},{3,21},{4,22},{5,23},{6,24},{7,25},{8,26},{9,... | collective-permute-start | bytes 98312
  815.9 18.0 %collective-permute-start.16 = (f32[16,512]{1,0:T(8,128)S(1)}, f32[16,512]{1,0:T(8,128)S(1)}, u32[]{:S(2)}, u32[]{:S(2)}) collective-permute-start(f32[16,512]{1,0:T(8,128)S(1)} %fusion), channel_id=1, source_target_pairs={{0,17},{1,18},{2,19},{3,20},{4,21},{5,22},{6,23},{7,24},{8,25},{9,... | collective-permute-start | bytes 98312
  817.8 21.2 %collective-permute-start.15 = (f32[16,512]{1,0:T(8,128)S(1)}, f32[16,512]{1,0:T(8,128)S(1)}, u32[]{:S(2)}, u32[]{:S(2)}) collective-permute-start(f32[16,512]{1,0:T(8,128)S(1)} %fusion), channel_id=1, source_target_pairs={{0,16},{1,17},{2,18},{3,19},{4,20},{5,21},{6,22},{7,23},{8,24},{9,... | collective-permute-start | bytes 98312
  824.6 19.1 %collective-permute-start.14 = (f32[16,512]{1,0:T(8,128)S(1)}, f32[16,512]{1,0:T(8,128)S(1)}, u32[]{:S(2)}, u32[]{:S(2)}) collective-permute-start(f32[16,512]{1,0:T(8,128)S(1)} %fusion), channel_id=1, source_target_pairs={{0,15},{1,16},{2,17},{3,18},{4,19},{5,20},{6,21},{7,22},{8,23},{9,... | collective-permute-start | bytes 98312
  827.7 19.4 %collective-permute-start.13 = (f32[16,512]{1,0:T(8,128)S(1)}, f32[16,512]{1,0:T(8,128)S(1)}, u32[]{:S(2)}, u32[]{:S(2)}) collective-permute-start(f32[16,512]{1,0:T(8,128)S(1)} %fusion), channel_id=1, source_target_pairs={{0,14},{1,15},{2,16},{3,17},{4,18},{5,19},{6,20},{7,21},{8,22},{9,... | collective-permute-start | bytes 98312
  829.7 19.4 %collective-permute-start.12 = (f32[16,512]{1,0:T(8,128)S(1)}, f32[16,512]{1,0:T(8,128)S(1)}, u32[]{:S(2)}, u32[]{:S(2)}) collective-permute-start(f32[16,512]{1,0:T(8,128)S(1)} %fusion), channel_id=1, source_target_pairs={{0,13},{1,14},{2,15},{3,16},{4,17},{5,18},{6,19},{7,20},{8,21},{9,... | collective-permute-start | bytes 98312
  833.9 17.1 %collective-permute-start.11 = (f32[16,512]{1,0:T(8,128)S(1)}, f32[16,512]{1,0:T(8,128)S(1)}, u32[]{:S(2)}, u32[]{:S(2)}) collective-permute-start(f32[16,512]{1,0:T(8,128)S(1)} %fusion), channel_id=1, source_target_pairs={{0,12},{1,13},{2,14},{3,15},{4,16},{5,17},{6,18},{7,19},{8,20},{9,... | collective-permute-start | bytes 98312
  839.0 16.4 %collective-permute-start.10 = (f32[16,512]{1,0:T(8,128)S(1)}, f32[16,512]{1,0:T(8,128)S(1)}, u32[]{:S(2)}, u32[]{:S(2)}) collective-permute-start(f32[16,512]{1,0:T(8,128)S(1)} %fusion), channel_id=1, source_target_pairs={{0,11},{1,12},{2,13},{3,14},{4,15},{5,16},{6,17},{7,18},{8,19},{9,... | collective-permute-start | bytes 98312
  843.7 93.9 %collective-permute-start.9 = (f32[16,512]{1,0:T(8,128)S(1)}, f32[16,512]{1,0:T(8,128)S(1)}, u32[]{:S(2)}, u32[]{:S(2)}) collective-permute-start(f32[16,512]{1,0:T(8,128)S(1)} %fusion), channel_id=1, source_target_pairs={{0,10},{1,11},{2,12},{3,13},{4,14},{5,15},{6,16},{7,17},{8,18},{9,... | collective-permute-start | bytes 98312
  847.1 95.0 %collective-permute-start.8 = (f32[16,512]{1,0:T(8,128)S(1)}, f32[16,512]{1,0:T(8,128)S(1)}, u32[]{:S(2)}, u32[]{:S(2)}) collective-permute-start(f32[16,512]{1,0:T(8,128)S(1)} %fusion), channel_id=1, source_target_pairs={{0,9},{1,10},{2,11},{3,12},{4,13},{5,14},{6,15},{7,16},{8,17},{9,1... | collective-permute-start | bytes 98312
  849.1 97.5 %collective-permute-start.7 = (f32[16,512]{1,0:T(8,128)S(1)}, f32[16,512]{1,0:T(8,128)S(1)}, u32[]{:S(2)}, u32[]{:S(2)}) collective-permute-start(f32[16,512]{1,0:T(8,128)S(1)} %fusion), channel_id=1, source_target_pairs={{0,8},{1,9},{2,10},{3,11},{4,12},{5,13},{6,14},{7,15},{8,16},{9,17... | collective-permute-start | bytes 98312
  851.1 97.9 %collective-permute-start.6 = (f32[16,512]{1,0:T(8,128)S(1)}, f32[16,512]{1,0:T(8,128)S(1)}, u32[]{:S(2)}, u32[]{:S(2)}) collective-permute-start(f32[16,512]{1,0:T(8,128)S(1)} %fusion), channel_id=1, source_target_pairs={{0,7},{1,8},{2,9},{3,10},{4,11},{5,12},{6,13},{7,14},{8,15},{9,16}... | collective-permute-start | bytes 98312
  855.5 96.8 %collective-permute-start.5 = (f32[16,512]{1,0:T(8,128)S(1)}, f32[16,512]{1,0:T(8,128)S(1)}, u32[]{:S(2)}, u32[]{:S(2)}) collective-permute-start(f32[16,512]{1,0:T(8,128)S(1)} %fusion), channel_id=1, source_target_pairs={{0,6},{1,7},{2,8},{3,9},{4,10},{5,11},{6,12},{7,13},{8,14},{9,15},... | collective-permute-start | bytes 98312
  937.6 19.6 %collective-permute-start.4 = (f32[16,512]{1,0:T(8,128)S(1)}, f32[16,512]{1,0:T(8,128)S(1)}, u32[]{:S(2)}, u32[]{:S(2)}) collective-permute-start(f32[16,512]{1,0:T(8,128)S(1)} %fusion), channel_id=1, source_target_pairs={{0,5},{1,6},{2,7},{3,8},{4,9},{5,10},{6,11},{7,12},{8,13},{9,14},{... | collective-permute-start | bytes 98312
  942.1 15.2 %collective-permute-start.3 = (f32[16,512]{1,0:T(8,128)S(1)}, f32[16,512]{1,0:T(8,128)S(1)}, u32[]{:S(2)}, u32[]{:S(2)}) collective-permute-start(f32[16,512]{1,0:T(8,128)S(1)} %fusion), channel_id=1, source_target_pairs={{0,4},{1,5},{2,6},{3,7},{4,8},{5,9},{6,10},{7,11},{8,12},{9,13},{1... | collective-permute-start | bytes 98312
  946.6 11.9 %collective-permute-start.2 = (f32[16,512]{1,0:T(8,128)S(1)}, f32[16,512]{1,0:T(8,128)S(1)}, u32[]{:S(2)}, u32[]{:S(2)}) collective-permute-start(f32[16,512]{1,0:T(8,128)S(1)} %fusion), channel_id=1, source_target_pairs={{0,3},{1,4},{2,5},{3,6},{4,7},{5,8},{6,9},{7,10},{8,11},{9,12},{10... | collective-permute-start | bytes 98312
  949.0 10.4 %collective-permute-start.1 = (f32[16,512]{1,0:T(8,128)S(1)}, f32[16,512]{1,0:T(8,128)S(1)}, u32[]{:S(2)}, u32[]{:S(2)}) collective-permute-start(f32[16,512]{1,0:T(8,128)S(1)} %fusion), channel_id=1, source_target_pairs={{0,2},{1,3},{2,4},{3,5},{4,6},{5,7},{6,8},{7,9},{8,10},{9,11},{10,... | collective-permute-start | bytes 98312
  (8 other events, 84.5 us)
Sparse Core Ops, SparseCore 0:
  9.8 55.2 all-gather.1
  686.0 342.8 all-reduce.23
where the time goes:
time: 1040 us
  blocking collectives  708 us (68%)
  starting transfers between devices  183 us (18%)
  waiting for transfers between devices  89.5 us (9%)
  matrix products  18.4 us (2%)
  between operations  14.7 us (1%)
  other arithmetic  14.6 us (1%)
    unnamed x2, blocking collectives  677 us
    unnamed x33, starting transfers between devices  183 us
    unnamed x35, waiting for transfers between devices  72.1 us
    all_gather x1, blocking collectives, per_device(): mix_full = lax.all_gather(mix_weight, 'shard', axis=0, tiled=True)  30.8 us
  transfers between devices with their start and end apart: 34, of which 6 were waited for; matrix products, arithmetic and copies ran while one was open for 2% of the time, Pallas kernels for 0%

commit v1 on v0

--- a/solution.py
+++ b/solution.py
@@ -43,9 +43,18 @@
 def per_device(
     audio, cotangent, clip_lengths, conv_weight, mix_weight, conv_bias, alpha_in, alpha_mid
 ):
+
+    def _hold_works(mat, peer_axis):
+        return jnp.concatenate(
+            lax.all_to_all(
+                jnp.stack(tuple((mat for _ in range(lax.axis_size(peer_axis))))), peer_axis, 0, 0
+            ),
+            0,
+        )
+
     rows = audio.shape[0]
     same_clip_flags = clip_masks(clip_lengths[0], rows)
-    mix_full = lax.all_gather(mix_weight, "shard", axis=0, tiled=True)
+    mix_full = _hold_works(mix_weight, "shard")
     audio_f = audio.astype(jnp.float32)
     act_in, slope_in, dalpha_in = snake_parts(audio_f, alpha_in)
     first = act_in.astype(jnp.bfloat16)

time: 1040 us -> 1040 us (level)
  blocking collectives: 708 us -> 678 us
  waiting for transfers between devices: 89.5 us -> 118 us
    all_gather x1 -> x0, blocking collectives: 30.8 us -> none  [per_device(): mix_full = lax.all_gather(mix_weight, 'shard', axis=0, tiled=True)]
    all_gather x1, waiting for transfers between devices: 17.5 us -> 44.3 us  [per_device(): lax.all_gather(conv_weight, 'shard', axis=0, tiled=True)]
  transfers between devices with their start and end apart: 34 -> 35, of which waited for: 6 -> 6; matrix products, arithmetic and copies ran while one was open for 2% -> 3% of each run, Pallas kernels for 0% -> 0%
where the time goes in v1:
time: 1040 us
  blocking collectives  678 us (65%)
  starting transfers between devices  190 us (18%)
  waiting for transfers between devices  118 us (11%)
  matrix products  18.4 us (2%)
  between operations  14.8 us (1%)
  other arithmetic  11.7 us (1%)
    unnamed x2, blocking collectives  678 us
    unnamed x33, starting transfers between devices  181 us
    unnamed x35, waiting for transfers between devices  73.4 us
    all_gather x1, waiting for transfers between devices, per_device(): lax.all_gather(conv_weight, 'shard', axis=0, tiled=True)  44.3 us
  transfers between devices with their start and end apart: 35, of which 6 were waited for; matrix products, arithmetic and copies ran while one was open for 3% of the time, Pallas kernels for 0%

profile of v1, /device:TPU:2, one launch (start us, length us, event | category | flops | bytes accessed | tf_op | source)
XLA Modules:
  0.0 1040.4 jit_solution(2561881116739494562)
XLA Ops:
  9.6 8.5 all-to-all-start
  23.6 44.3 %all-gather.2.cloned.1.call-done = bf16[3584,512]{1,0:T(8,128)(2,1)} async-done(((bf16[448,512]{1,0:T(8,128)(2,1)}), bf16[3584,512]{1,0:T(8,128)(2,1)}) %all-gather.2.cloned.1.call-update) | async-done | bytes 3670032 | tf_op jit(solution)/shard_map/all_gather | solution.py:71
  67.9 3.1 convolution_add_fusion
  71.8 3.0 fusion.14
  74.8 4.9 convert_reduce_fusion.1
  79.8 4.1 fusion.23
  83.8 598.2 %fusion = f32[16,512]{1,0:T(8,128)S(1)} fusion(f32[3584,512]{1,0:T(8,128)} %fusion.23), kind=kCustom, calls=%all-reduce-scatter | all-reduce-scatter fusion | flops 2097153 | bytes 7372800
  689.8 3.3 convolution_convert_fusion
  693.2 2.9 collective-permute-start.31
  696.4 5.4 collective-permute-done.31
  701.9 50.8 %collective-permute-start.26 = (f32[16,512]{1,0:T(8,128)S(1)}, f32[16,512]{1,0:T(8,128)S(1)}, u32[]{:S(2)}, u32[]{:S(2)}) collective-permute-start(f32[16,512]{1,0:T(8,128)S(1)} %fusion), channel_id=1, source_target_pairs={{0,27},{1,28},{2,29},{3,30},{4,31},{5,32},{6,33},{7,34},{8,35},{9,... | collective-permute-start | bytes 98312
  756.7 43.3 %collective-permute-start.23 = (f32[16,512]{1,0:T(8,128)S(1)}, f32[16,512]{1,0:T(8,128)S(1)}, u32[]{:S(2)}, u32[]{:S(2)}) collective-permute-start(f32[16,512]{1,0:T(8,128)S(1)} %fusion), channel_id=1, source_target_pairs={{0,24},{1,25},{2,26},{3,27},{4,28},{5,29},{6,30},{7,31},{8,32},{9,... | collective-permute-start | bytes 98312
  800.0 3.4 collective-permute-start.22
  805.5 2.8 collective-permute-start.20
  808.4 5.1 collective-permute-start.19
  813.6 3.7 collective-permute-start.18
  821.2 2.8 collective-permute-start.15
  824.0 3.9 fusion.13
  827.9 3.2 collective-permute-start.14
  833.0 4.2 collective-permute-start.12
  837.3 5.1 collective-permute-start.11
  844.5 2.5 convert_reduce_fusion
  847.0 3.4 collective-permute-start.9
  854.4 4.4 collective-permute-start.6
  860.9 80.1 %all-reduce.20 = f32[4,512]{1,0:T(4,128)S(1)} all-reduce(f32[4,512]{1,0:T(4,128)S(1)} %pad_maximum_fusion), channel_id=4, replica_groups=mesh['dp'=32,'shard'=8] {'dp','shard'}, use_global_device_ids=true, to_apply=%region_8.9.clone | all-reduce | flops 2048 | bytes 16384
  940.9 4.5 collective-permute-start.4
  945.4 4.5 collective-permute-start.3
  952.3 3.3 collective-permute-start.1
  955.6 4.2 collective-permute-start
  962.7 3.0 collective-permute-done
  965.7 3.8 concatenate.76
  970.2 62.1 %all-reduce.24.cloned.1.call-done = f32[512,512]{1,0:T(8,128)} async-done(((f32[512,512]{1,0:T(8,128)}), f32[512,512]{1,0:T(8,128)}) %all-reduce.24.cloned.1.call-update) | async-done | bytes 1048592
  (99 shorter events, 43.9 us)
Async XLA Ops:
  7.2 60.7 %all-gather.2.cloned.1.call-start = ((), (), s32[]{:S(2)}) async-start(), calls=%async_computation.1 | async-start | bytes 4128768 | tf_op jit(solution)/shard_map/all_gather | solution.py:71
  9.6 65.2 %all-to-all-start = ((bf16[8,64,512]{2,1,0:T(8,128)(2,1)}), bf16[8,64,512]{2,1,0:T(8,128)(2,1)S(1)}, u32[]{:S(2)}, u32[]{:S(2)}) async-start(bf16[8,64,512]{2,1,0:T(8,128)(2,1)} %stack.12), calls=%async_computation | async-start | bytes 1048576 | tf_op jit(solution)/shard_map/all_to_all | solution.py:49
  18.1 1014.2 %all-reduce.24.cloned.1.call-start = ((), (), s32[]{:S(2)}) async-start(), calls=%async_computation.2 | async-start | bytes 2097152
  682.0 70.7 %collective-permute-start.30 = (f32[16,512]{1,0:T(8,128)S(1)}, f32[16,512]{1,0:T(8,128)S(1)}, u32[]{:S(2)}, u32[]{:S(2)}) collective-permute-start(f32[16,512]{1,0:T(8,128)S(1)} %fusion), channel_id=1, source_target_pairs={{0,31},{1,32},{2,33},{3,34},{4,35},{5,36},{6,37},{7,38},{8,39},{9,... | collective-permute-start | bytes 98312
  684.0 70.8 %collective-permute-start.29 = (f32[16,512]{1,0:T(8,128)S(1)}, f32[16,512]{1,0:T(8,128)S(1)}, u32[]{:S(2)}, u32[]{:S(2)}) collective-permute-start(f32[16,512]{1,0:T(8,128)S(1)} %fusion), channel_id=1, source_target_pairs={{0,30},{1,31},{2,32},{3,33},{4,34},{5,35},{6,36},{7,37},{8,38},{9,... | collective-permute-start | bytes 98312
  685.9 70.8 %collective-permute-start.28 = (f32[16,512]{1,0:T(8,128)S(1)}, f32[16,512]{1,0:T(8,128)S(1)}, u32[]{:S(2)}, u32[]{:S(2)}) collective-permute-start(f32[16,512]{1,0:T(8,128)S(1)} %fusion), channel_id=1, source_target_pairs={{0,29},{1,30},{2,31},{3,32},{4,33},{5,34},{6,35},{7,36},{8,37},{9,... | collective-permute-start | bytes 98312
  687.8 112.2 %collective-permute-start.27 = (f32[16,512]{1,0:T(8,128)S(1)}, f32[16,512]{1,0:T(8,128)S(1)}, u32[]{:S(2)}, u32[]{:S(2)}) collective-permute-start(f32[16,512]{1,0:T(8,128)S(1)} %fusion), channel_id=1, source_target_pairs={{0,28},{1,29},{2,30},{3,31},{4,32},{5,33},{6,34},{7,35},{8,36},{9,... | collective-permute-start | bytes 98312
  701.9 101.6 %collective-permute-start.26 = (f32[16,512]{1,0:T(8,128)S(1)}, f32[16,512]{1,0:T(8,128)S(1)}, u32[]{:S(2)}, u32[]{:S(2)}) collective-permute-start(f32[16,512]{1,0:T(8,128)S(1)} %fusion), channel_id=1, source_target_pairs={{0,27},{1,28},{2,29},{3,30},{4,31},{5,32},{6,33},{7,34},{8,35},{9,... | collective-permute-start | bytes 98312
  752.7 52.8 %collective-permute-start.25 = (f32[16,512]{1,0:T(8,128)S(1)}, f32[16,512]{1,0:T(8,128)S(1)}, u32[]{:S(2)}, u32[]{:S(2)}) collective-permute-start(f32[16,512]{1,0:T(8,128)S(1)} %fusion), channel_id=1, source_target_pairs={{0,26},{1,27},{2,28},{3,29},{4,30},{5,31},{6,32},{7,33},{8,34},{9,... | collective-permute-start | bytes 98312
  754.8 53.7 %collective-permute-start.24 = (f32[16,512]{1,0:T(8,128)S(1)}, f32[16,512]{1,0:T(8,128)S(1)}, u32[]{:S(2)}, u32[]{:S(2)}) collective-permute-start(f32[16,512]{1,0:T(8,128)S(1)} %fusion), channel_id=1, source_target_pairs={{0,25},{1,26},{2,27},{3,28},{4,29},{5,30},{6,31},{7,32},{8,33},{9,... | collective-permute-start | bytes 98312
  756.7 56.9 %collective-permute-start.23 = (f32[16,512]{1,0:T(8,128)S(1)}, f32[16,512]{1,0:T(8,128)S(1)}, u32[]{:S(2)}, u32[]{:S(2)}) collective-permute-start(f32[16,512]{1,0:T(8,128)S(1)} %fusion), channel_id=1, source_target_pairs={{0,24},{1,25},{2,26},{3,27},{4,28},{5,29},{6,30},{7,31},{8,32},{9,... | collective-permute-start | bytes 98312
  800.0 17.2 %collective-permute-start.22 = (f32[16,512]{1,0:T(8,128)S(1)}, f32[16,512]{1,0:T(8,128)S(1)}, u32[]{:S(2)}, u32[]{:S(2)}) collective-permute-start(f32[16,512]{1,0:T(8,128)S(1)} %fusion), channel_id=1, source_target_pairs={{0,23},{1,24},{2,25},{3,26},{4,27},{5,28},{6,29},{7,30},{8,31},{9,... | collective-permute-start | bytes 98312
  803.5 15.8 %collective-permute-start.21 = (f32[16,512]{1,0:T(8,128)S(1)}, f32[16,512]{1,0:T(8,128)S(1)}, u32[]{:S(2)}, u32[]{:S(2)}) collective-permute-start(f32[16,512]{1,0:T(8,128)S(1)} %fusion), channel_id=1, source_target_pairs={{0,22},{1,23},{2,24},{3,25},{4,26},{5,27},{6,28},{7,29},{8,30},{9,... | collective-permute-start | bytes 98312
  805.5 15.7 %collective-permute-start.20 = (f32[16,512]{1,0:T(8,128)S(1)}, f32[16,512]{1,0:T(8,128)S(1)}, u32[]{:S(2)}, u32[]{:S(2)}) collective-permute-start(f32[16,512]{1,0:T(8,128)S(1)} %fusion), channel_id=1, source_target_pairs={{0,21},{1,22},{2,23},{3,24},{4,25},{5,26},{6,27},{7,28},{8,29},{9,... | collective-permute-start | bytes 98312
  808.4 19.5 %collective-permute-start.19 = (f32[16,512]{1,0:T(8,128)S(1)}, f32[16,512]{1,0:T(8,128)S(1)}, u32[]{:S(2)}, u32[]{:S(2)}) collective-permute-start(f32[16,512]{1,0:T(8,128)S(1)} %fusion), channel_id=1, source_target_pairs={{0,20},{1,21},{2,22},{3,23},{4,24},{5,25},{6,26},{7,27},{8,28},{9,... | collective-permute-start | bytes 98312
  813.6 17.5 %collective-permute-start.18 = (f32[16,512]{1,0:T(8,128)S(1)}, f32[16,512]{1,0:T(8,128)S(1)}, u32[]{:S(2)}, u32[]{:S(2)}) collective-permute-start(f32[16,512]{1,0:T(8,128)S(1)} %fusion), channel_id=1, source_target_pairs={{0,19},{1,20},{2,21},{3,22},{4,23},{5,24},{6,25},{7,26},{8,27},{9,... | collective-permute-start | bytes 98312
  817.3 15.7 %collective-permute-start.17 = (f32[16,512]{1,0:T(8,128)S(1)}, f32[16,512]{1,0:T(8,128)S(1)}, u32[]{:S(2)}, u32[]{:S(2)}) collective-permute-start(f32[16,512]{1,0:T(8,128)S(1)} %fusion), channel_id=1, source_target_pairs={{0,18},{1,19},{2,20},{3,21},{4,22},{5,23},{6,24},{7,25},{8,26},{9,... | collective-permute-start | bytes 98312
  819.2 18.0 %collective-permute-start.16 = (f32[16,512]{1,0:T(8,128)S(1)}, f32[16,512]{1,0:T(8,128)S(1)}, u32[]{:S(2)}, u32[]{:S(2)}) collective-permute-start(f32[16,512]{1,0:T(8,128)S(1)} %fusion), channel_id=1, source_target_pairs={{0,17},{1,18},{2,19},{3,20},{4,21},{5,22},{6,23},{7,24},{8,25},{9,... | collective-permute-start | bytes 98312
  821.2 21.2 %collective-permute-start.15 = (f32[16,512]{1,0:T(8,128)S(1)}, f32[16,512]{1,0:T(8,128)S(1)}, u32[]{:S(2)}, u32[]{:S(2)}) collective-permute-start(f32[16,512]{1,0:T(8,128)S(1)} %fusion), channel_id=1, source_target_pairs={{0,16},{1,17},{2,18},{3,19},{4,20},{5,21},{6,22},{7,23},{8,24},{9,... | collective-permute-start | bytes 98312
  827.9 19.1 %collective-permute-start.14 = (f32[16,512]{1,0:T(8,128)S(1)}, f32[16,512]{1,0:T(8,128)S(1)}, u32[]{:S(2)}, u32[]{:S(2)}) collective-permute-start(f32[16,512]{1,0:T(8,128)S(1)} %fusion), channel_id=1, source_target_pairs={{0,15},{1,16},{2,17},{3,18},{4,19},{5,20},{6,21},{7,22},{8,23},{9,... | collective-permute-start | bytes 98312
  831.1 19.3 %collective-permute-start.13 = (f32[16,512]{1,0:T(8,128)S(1)}, f32[16,512]{1,0:T(8,128)S(1)}, u32[]{:S(2)}, u32[]{:S(2)}) collective-permute-start(f32[16,512]{1,0:T(8,128)S(1)} %fusion), channel_id=1, source_target_pairs={{0,14},{1,15},{2,16},{3,17},{4,18},{5,19},{6,20},{7,21},{8,22},{9,... | collective-permute-start | bytes 98312
  833.0 19.4 %collective-permute-start.12 = (f32[16,512]{1,0:T(8,128)S(1)}, f32[16,512]{1,0:T(8,128)S(1)}, u32[]{:S(2)}, u32[]{:S(2)}) collective-permute-start(f32[16,512]{1,0:T(8,128)S(1)} %fusion), channel_id=1, source_target_pairs={{0,13},{1,14},{2,15},{3,16},{4,17},{5,18},{6,19},{7,20},{8,21},{9,... | collective-permute-start | bytes 98312
  837.3 17.1 %collective-permute-start.11 = (f32[16,512]{1,0:T(8,128)S(1)}, f32[16,512]{1,0:T(8,128)S(1)}, u32[]{:S(2)}, u32[]{:S(2)}) collective-permute-start(f32[16,512]{1,0:T(8,128)S(1)} %fusion), channel_id=1, source_target_pairs={{0,12},{1,13},{2,14},{3,15},{4,16},{5,17},{6,18},{7,19},{8,20},{9,... | collective-permute-start | bytes 98312
  842.4 16.4 %collective-permute-start.10 = (f32[16,512]{1,0:T(8,128)S(1)}, f32[16,512]{1,0:T(8,128)S(1)}, u32[]{:S(2)}, u32[]{:S(2)}) collective-permute-start(f32[16,512]{1,0:T(8,128)S(1)} %fusion), channel_id=1, source_target_pairs={{0,11},{1,12},{2,13},{3,14},{4,15},{5,16},{6,17},{7,18},{8,19},{9,... | collective-permute-start | bytes 98312
  847.0 93.9 %collective-permute-start.9 = (f32[16,512]{1,0:T(8,128)S(1)}, f32[16,512]{1,0:T(8,128)S(1)}, u32[]{:S(2)}, u32[]{:S(2)}) collective-permute-start(f32[16,512]{1,0:T(8,128)S(1)} %fusion), channel_id=1, source_target_pairs={{0,10},{1,11},{2,12},{3,13},{4,14},{5,15},{6,16},{7,17},{8,18},{9,... | collective-permute-start | bytes 98312
  850.4 95.0 %collective-permute-start.8 = (f32[16,512]{1,0:T(8,128)S(1)}, f32[16,512]{1,0:T(8,128)S(1)}, u32[]{:S(2)}, u32[]{:S(2)}) collective-permute-start(f32[16,512]{1,0:T(8,128)S(1)} %fusion), channel_id=1, source_target_pairs={{0,9},{1,10},{2,11},{3,12},{4,13},{5,14},{6,15},{7,16},{8,17},{9,1... | collective-permute-start | bytes 98312
  852.4 97.5 %collective-permute-start.7 = (f32[16,512]{1,0:T(8,128)S(1)}, f32[16,512]{1,0:T(8,128)S(1)}, u32[]{:S(2)}, u32[]{:S(2)}) collective-permute-start(f32[16,512]{1,0:T(8,128)S(1)} %fusion), channel_id=1, source_target_pairs={{0,8},{1,9},{2,10},{3,11},{4,12},{5,13},{6,14},{7,15},{8,16},{9,17... | collective-permute-start | bytes 98312
  854.4 97.9 %collective-permute-start.6 = (f32[16,512]{1,0:T(8,128)S(1)}, f32[16,512]{1,0:T(8,128)S(1)}, u32[]{:S(2)}, u32[]{:S(2)}) collective-permute-start(f32[16,512]{1,0:T(8,128)S(1)} %fusion), channel_id=1, source_target_pairs={{0,7},{1,8},{2,9},{3,10},{4,11},{5,12},{6,13},{7,14},{8,15},{9,16}... | collective-permute-start | bytes 98312
  858.8 96.8 %collective-permute-start.5 = (f32[16,512]{1,0:T(8,128)S(1)}, f32[16,512]{1,0:T(8,128)S(1)}, u32[]{:S(2)}, u32[]{:S(2)}) collective-permute-start(f32[16,512]{1,0:T(8,128)S(1)} %fusion), channel_id=1, source_target_pairs={{0,6},{1,7},{2,8},{3,9},{4,10},{5,11},{6,12},{7,13},{8,14},{9,15},... | collective-permute-start | bytes 98312
  940.9 19.7 %collective-permute-start.4 = (f32[16,512]{1,0:T(8,128)S(1)}, f32[16,512]{1,0:T(8,128)S(1)}, u32[]{:S(2)}, u32[]{:S(2)}) collective-permute-start(f32[16,512]{1,0:T(8,128)S(1)} %fusion), channel_id=1, source_target_pairs={{0,5},{1,6},{2,7},{3,8},{4,9},{5,10},{6,11},{7,12},{8,13},{9,14},{... | collective-permute-start | bytes 98312
  945.4 15.2 %collective-permute-start.3 = (f32[16,512]{1,0:T(8,128)S(1)}, f32[16,512]{1,0:T(8,128)S(1)}, u32[]{:S(2)}, u32[]{:S(2)}) collective-permute-start(f32[16,512]{1,0:T(8,128)S(1)} %fusion), channel_id=1, source_target_pairs={{0,4},{1,5},{2,6},{3,7},{4,8},{5,9},{6,10},{7,11},{8,12},{9,13},{1... | collective-permute-start | bytes 98312
  950.0 11.9 %collective-permute-start.2 = (f32[16,512]{1,0:T(8,128)S(1)}, f32[16,512]{1,0:T(8,128)S(1)}, u32[]{:S(2)}, u32[]{:S(2)}) collective-permute-start(f32[16,512]{1,0:T(8,128)S(1)} %fusion), channel_id=1, source_target_pairs={{0,3},{1,4},{2,5},{3,6},{4,7},{5,8},{6,9},{7,10},{8,11},{9,12},{10... | collective-permute-start | bytes 98312
  (10 other events, 161.8 us)
Sparse Core Ops, SparseCore 0:
  9.8 58.0 all-gather.1
  689.9 342.3 all-reduce.23
